TPU v7x, 256 devices: a whole 4x4x8 slice. The times are simulated.
256 devices in a mesh: row: 8 (over z_hi, x), col: 32 (over z_lo, y, core).
Axes of the slice: x: 4, y: 4, z: 8 (z_hi: 2, z_lo: 4; z = z_hi * 4 + z_lo), core: 2. Of those that a mesh axis runs over, the one named last changes fastest.
Arguments:
- region_factors: bfloat16 [262144, 512], P(('row', 'col')), may hold values from -1.25 to 1.25
- item_factors: bfloat16 [32, 128, 512], P('col', 'row'), may hold values from -1.25 to 1.25
- slab_blocks: bfloat16 [256, 32, 6, 128, 128], P(('row', 'col')), may hold values from -6 to 6
- block_rows: int32 [256, 32, 6], P(('row', 'col')), may hold values from 0 to 7, as said below
- counts: int32 [256, 32], P(('row', 'col')), may hold values from 1 to 6, as said below
Outputs:
- new_regions: float32 [262144, 512], P(('row', 'col'))
- new_items: float32 [32, 128, 512], P('col', 'row')
Inputs may be any that keep to these rules, and one draw needn't show every extreme that they name: `counts`: every entry is at least 1; some device-block has exactly 6 present blocks in some block column. `block_rows`: for each device-block and block column, the first counts[d, p] entries are distinct; entries at slots s >= counts[d, p] (and their slab blocks) are not used.
All inputs are finite; a program needn't handle non-finite values.
Results may differ from a plain program's by a relative error of at most 0.0023.
Values may be sent and summed in bfloat16 or wider, within the bound.
No kernel may reach another device: no remote copies, remote signals or barrier semaphores. Data moves between devices by JAX's collectives and lax.ppermute only.
A program may use at most 128 MiB of HBM per device.

v0:
```python
import jax
import jax.numpy as jnp
from jax import lax
from jax.sharding import PartitionSpec as P

region_rate = 0.05
item_rate = 0.01
decay_rate = 0.1


def passed_along(value, axis, steps):
    count = lax.axis_size(axis)
    pairs = [(source, (source + steps) % count) for source in range(count)]
    return lax.ppermute(value, axis, pairs)


def pass_panel(panel_now):
    return passed_along(panel_now, "col", 1)


def on_device(region_factors, item_factors, slab_blocks, block_rows, counts):
    cycle_size = lax.axis_size("col")
    position = lax.axis_index("col")
    block_size = slab_blocks.shape[-1]
    factor_width = region_factors.shape[-1]
    slot_total = slab_blocks.shape[2]
    row_blocks = region_factors.shape[0] // block_size
    region_blocks = region_factors.reshape(row_blocks, block_size, factor_width)
    tiles_all = slab_blocks[0]
    row_lists = block_rows[0]
    live_counts = counts[0]
    slot_ids = jnp.arange(slot_total, dtype=jnp.int32)
    panel_start = lax.all_gather(item_factors, "row", axis=1, tiled=True)[0]
    region_zero = jnp.zeros((row_blocks, block_size, factor_width), jnp.float32)
    item_zero = jnp.zeros((block_size, factor_width), jnp.float32)

    def padded_work(column, panel_now, region_totals):
        rows_now = lax.dynamic_index_in_dim(row_lists, column, 0, keepdims=False)
        tiles_now = lax.dynamic_index_in_dim(tiles_all, column, 0, keepdims=False)
        count_now = lax.dynamic_index_in_dim(live_counts, column, 0, keepdims=False)
        chosen = jnp.take(region_blocks, rows_now, axis=0)
        predicted = jnp.einsum("sik,jk->sij", chosen, panel_now, preferred_element_type=jnp.float32)
        present = slot_ids < count_now
        residual = jnp.where(present[:, None, None], predicted - tiles_now.astype(jnp.float32), 0.0)
        residual = residual.astype(jnp.bfloat16)
        update = jnp.einsum("sij,jk->sik", residual, panel_now, preferred_element_type=jnp.float32)
        region_totals = region_totals.at[rows_now].add(update)
        item_part = jnp.einsum("sij,sik->jk", residual, chosen, preferred_element_type=jnp.float32)
        return (region_totals, item_part)

    def block_work(column, panel_now, region_totals):
        return padded_work(column, panel_now, region_totals)

    last_column = (position + 1) % cycle_size

    def cycle_travel(passed, carried):
        panel_now, grad_now, region_totals = carried
        column = (position - passed) % cycle_size
        region_totals, item_part = block_work(column, panel_now, region_totals)
        grad_now = grad_now + item_part
        panel_now = pass_panel(panel_now)
        grad_now = passed_along(grad_now, "col", 1)
        return (panel_now, grad_now, region_totals)

    panel_now, grad_now, region_totals = lax.fori_loop(
        0, cycle_size - 1, cycle_travel, (panel_start, item_zero, region_zero)
    )
    region_totals, item_part = block_work(last_column, panel_now, region_totals)
    grad_home = passed_along(grad_now + item_part, "col", 1)
    own_piece = lax.psum_scatter(grad_home, "row", scatter_dimension=0, tiled=True)
    regions_wide = region_factors.astype(jnp.float32)
    region_grad = region_totals.reshape(row_blocks * block_size, factor_width)
    new_regions = regions_wide - region_rate * (region_grad + decay_rate * regions_wide)
    own_rows = item_factors[0].astype(jnp.float32)
    new_items = (own_rows - item_rate * (own_piece + decay_rate * own_rows))[None]
    return (new_regions, new_items)


def solution(mesh):
    return jax.shard_map(
        on_device,
        mesh=mesh,
        in_specs=(
            P(("row", "col"), None),
            P("col", "row", None),
            P(("row", "col"), None, None, None, None),
            P(("row", "col"), None, None),
            P(("row", "col"), None),
        ),
        out_specs=(P(("row", "col"), None), P("col", "row", None)),
        check_vma=False,
    )
```

profile of v0, /device:TPU:32, one launch (start us, length us, event | category | flops | bytes accessed | tf_op | source)
XLA Modules:
  0.0 606.1 jit_solution(15959370318166916743)
XLA Ops:
  11.0 45.3 %all_gather.3 = bf16[1,128,512]{2,1,0:T(8,128)(2,1)S(1)} all-gather(bf16[1,16,512]{2,1,0:T(8,128)(2,1)} %param.10), channel_id=1, replica_groups=mesh['row'=8,'col'=32] {'row'}, dimensions={1}, use_global_device_ids=true | all-gather | bytes 147456 | tf_op jit(solution)/shard_map/all_gather | solution.py:33
  60.6 393.8 %while.20 = (s32[]{:T(128)}, bf16[128,512]{1,0:T(8,128)(2,1)S(1)}, f32[128,512]{1,0:T(8,128)S(1)}, f32[8,128,512]{2,1,0:T(8,128)}, s32[]{:T(128)}, /*index=5*/s3...) while((s32[]{:T(128)}, bf16[128,512]{1,0:T(8,128)(2,1)S(1)}, ...), condition=%wide.region_2.4_spmd.clone, body=%wide.region_0.3_spmd.clone.sunk | while | flops 303629376 | bytes 12849738 | solution.py:65
  67.0 3.9 scatter_fusion
  77.9 3.9 scatter_fusion
  90.4 3.9 scatter_fusion
  103.0 3.9 scatter_fusion
  115.5 3.9 scatter_fusion
  128.0 3.9 scatter_fusion
  140.6 3.9 scatter_fusion
  153.1 3.9 scatter_fusion
  165.6 3.9 scatter_fusion
  178.2 3.9 scatter_fusion
  190.7 3.9 scatter_fusion
  203.2 3.9 scatter_fusion
  215.8 3.9 scatter_fusion
  228.3 3.9 scatter_fusion
  240.8 3.9 scatter_fusion
  253.4 3.9 scatter_fusion
  265.9 3.9 scatter_fusion
  278.4 3.9 scatter_fusion
  291.0 3.9 scatter_fusion
  303.5 3.9 scatter_fusion
  316.0 3.9 scatter_fusion
  341.1 3.9 scatter_fusion
  393.2 3.9 scatter_fusion
  415.9 5.4 collective-permute-start.1
  430.1 5.6 collective-permute-start.1
  436.1 3.9 scatter_fusion
  444.4 5.7 collective-permute-start.1
  450.5 3.9 scatter_fusion
  458.2 6.7 %collective-permute-done.2 = f32[128,512]{1,0:T(8,128)S(1)} collective-permute-done((f32[128,512]{1,0:T(8,128)S(1)}, f32[128,512]{1,0:T(8,128)S(1)}, u32[]{:S(2)}, u32[]{:S(2)}) %collective-permute-start.2) | collective-permute-done | bytes 262176 | tf_op jit(solution)/shard_map/ppermute | solution.py:14
  470.3 127.5 %reduce-scatter.2.cloned.1.call-done = f32[16,512]{1,0:T(8,128)} async-done(((f32[128,512]{1,0:T(8,128)}), f32[16,512]{1,0:T(8,128)}) %reduce-scatter.2.cloned.1.call-update) | async-done | bytes 32784 | tf_op jit(solution)/shard_map/reduce_scatter | solution.py:70
  (468 shorter events, 295.5 us)
Async XLA Ops:
  7.2 590.6 %reduce-scatter.2.cloned.1.call-start = ((), (), s32[]{:S(2)}) async-start(), calls=%async_computation.1 | async-start | bytes 294912 | tf_op jit(solution)/shard_map/reduce_scatter | solution.py:70
  60.6 10.3 %collective-permute-start = (bf16[128,512]{1,0:T(8,128)(2,1)S(1)}, bf16[128,512]{1,0:T(8,128)(2,1)S(1)}, u32[]{:S(2)}, u32[]{:S(2)}) collective-permute-start(bf16[128,512]{1,0:T(8,128)(2,1)S(1)} %copy.21), channel_id=1, source_target_pairs={{0,1},{1,2},{2,3},{3,4},{4,5},{5,6},{6,7},{7,8},{8,9},{9,10},{10,1... | collective-permute-start | bytes 393224 | tf_op jit(solution)/shard_map/while/body/eval_jaxpr/ppermute | solution.py:14
  73.1 8.7 %collective-permute-start = (bf16[128,512]{1,0:T(8,128)(2,1)S(1)}, bf16[128,512]{1,0:T(8,128)(2,1)S(1)}, u32[]{:S(2)}, u32[]{:S(2)}) collective-permute-start(bf16[128,512]{1,0:T(8,128)(2,1)S(1)} %copy.21), channel_id=1, source_target_pairs={{0,1},{1,2},{2,3},{3,4},{4,5},{5,6},{6,7},{7,8},{8,9},{9,10},{10,1... | collective-permute-start | bytes 393224 | tf_op jit(solution)/shard_map/while/body/eval_jaxpr/ppermute | solution.py:14
  85.7 8.7 %collective-permute-start = (bf16[128,512]{1,0:T(8,128)(2,1)S(1)}, bf16[128,512]{1,0:T(8,128)(2,1)S(1)}, u32[]{:S(2)}, u32[]{:S(2)}) collective-permute-start(bf16[128,512]{1,0:T(8,128)(2,1)S(1)} %copy.21), channel_id=1, source_target_pairs={{0,1},{1,2},{2,3},{3,4},{4,5},{5,6},{6,7},{7,8},{8,9},{9,10},{10,1... | collective-permute-start | bytes 393224 | tf_op jit(solution)/shard_map/while/body/eval_jaxpr/ppermute | solution.py:14
  98.2 8.7 %collective-permute-start = (bf16[128,512]{1,0:T(8,128)(2,1)S(1)}, bf16[128,512]{1,0:T(8,128)(2,1)S(1)}, u32[]{:S(2)}, u32[]{:S(2)}) collective-permute-start(bf16[128,512]{1,0:T(8,128)(2,1)S(1)} %copy.21), channel_id=1, source_target_pairs={{0,1},{1,2},{2,3},{3,4},{4,5},{5,6},{6,7},{7,8},{8,9},{9,10},{10,1... | collective-permute-start | bytes 393224 | tf_op jit(solution)/shard_map/while/body/eval_jaxpr/ppermute | solution.py:14
  110.7 8.7 %collective-permute-start = (bf16[128,512]{1,0:T(8,128)(2,1)S(1)}, bf16[128,512]{1,0:T(8,128)(2,1)S(1)}, u32[]{:S(2)}, u32[]{:S(2)}) collective-permute-start(bf16[128,512]{1,0:T(8,128)(2,1)S(1)} %copy.21), channel_id=1, source_target_pairs={{0,1},{1,2},{2,3},{3,4},{4,5},{5,6},{6,7},{7,8},{8,9},{9,10},{10,1... | collective-permute-start | bytes 393224 | tf_op jit(solution)/shard_map/while/body/eval_jaxpr/ppermute | solution.py:14
  123.3 8.7 %collective-permute-start = (bf16[128,512]{1,0:T(8,128)(2,1)S(1)}, bf16[128,512]{1,0:T(8,128)(2,1)S(1)}, u32[]{:S(2)}, u32[]{:S(2)}) collective-permute-start(bf16[128,512]{1,0:T(8,128)(2,1)S(1)} %copy.21), channel_id=1, source_target_pairs={{0,1},{1,2},{2,3},{3,4},{4,5},{5,6},{6,7},{7,8},{8,9},{9,10},{10,1... | collective-permute-start | bytes 393224 | tf_op jit(solution)/shard_map/while/body/eval_jaxpr/ppermute | solution.py:14
  135.8 8.7 %collective-permute-start = (bf16[128,512]{1,0:T(8,128)(2,1)S(1)}, bf16[128,512]{1,0:T(8,128)(2,1)S(1)}, u32[]{:S(2)}, u32[]{:S(2)}) collective-permute-start(bf16[128,512]{1,0:T(8,128)(2,1)S(1)} %copy.21), channel_id=1, source_target_pairs={{0,1},{1,2},{2,3},{3,4},{4,5},{5,6},{6,7},{7,8},{8,9},{9,10},{10,1... | collective-permute-start | bytes 393224 | tf_op jit(solution)/shard_map/while/body/eval_jaxpr/ppermute | solution.py:14
  148.3 8.7 %collective-permute-start = (bf16[128,512]{1,0:T(8,128)(2,1)S(1)}, bf16[128,512]{1,0:T(8,128)(2,1)S(1)}, u32[]{:S(2)}, u32[]{:S(2)}) collective-permute-start(bf16[128,512]{1,0:T(8,128)(2,1)S(1)} %copy.21), channel_id=1, source_target_pairs={{0,1},{1,2},{2,3},{3,4},{4,5},{5,6},{6,7},{7,8},{8,9},{9,10},{10,1... | collective-permute-start | bytes 393224 | tf_op jit(solution)/shard_map/while/body/eval_jaxpr/ppermute | solution.py:14
  160.9 8.7 %collective-permute-start = (bf16[128,512]{1,0:T(8,128)(2,1)S(1)}, bf16[128,512]{1,0:T(8,128)(2,1)S(1)}, u32[]{:S(2)}, u32[]{:S(2)}) collective-permute-start(bf16[128,512]{1,0:T(8,128)(2,1)S(1)} %copy.21), channel_id=1, source_target_pairs={{0,1},{1,2},{2,3},{3,4},{4,5},{5,6},{6,7},{7,8},{8,9},{9,10},{10,1... | collective-permute-start | bytes 393224 | tf_op jit(solution)/shard_map/while/body/eval_jaxpr/ppermute | solution.py:14
  173.4 8.7 %collective-permute-start = (bf16[128,512]{1,0:T(8,128)(2,1)S(1)}, bf16[128,512]{1,0:T(8,128)(2,1)S(1)}, u32[]{:S(2)}, u32[]{:S(2)}) collective-permute-start(bf16[128,512]{1,0:T(8,128)(2,1)S(1)} %copy.21), channel_id=1, source_target_pairs={{0,1},{1,2},{2,3},{3,4},{4,5},{5,6},{6,7},{7,8},{8,9},{9,10},{10,1... | collective-permute-start | bytes 393224 | tf_op jit(solution)/shard_map/while/body/eval_jaxpr/ppermute | solution.py:14
  185.9 8.7 %collective-permute-start = (bf16[128,512]{1,0:T(8,128)(2,1)S(1)}, bf16[128,512]{1,0:T(8,128)(2,1)S(1)}, u32[]{:S(2)}, u32[]{:S(2)}) collective-permute-start(bf16[128,512]{1,0:T(8,128)(2,1)S(1)} %copy.21), channel_id=1, source_target_pairs={{0,1},{1,2},{2,3},{3,4},{4,5},{5,6},{6,7},{7,8},{8,9},{9,10},{10,1... | collective-permute-start | bytes 393224 | tf_op jit(solution)/shard_map/while/body/eval_jaxpr/ppermute | solution.py:14
  198.5 8.7 %collective-permute-start = (bf16[128,512]{1,0:T(8,128)(2,1)S(1)}, bf16[128,512]{1,0:T(8,128)(2,1)S(1)}, u32[]{:S(2)}, u32[]{:S(2)}) collective-permute-start(bf16[128,512]{1,0:T(8,128)(2,1)S(1)} %copy.21), channel_id=1, source_target_pairs={{0,1},{1,2},{2,3},{3,4},{4,5},{5,6},{6,7},{7,8},{8,9},{9,10},{10,1... | collective-permute-start | bytes 393224 | tf_op jit(solution)/shard_map/while/body/eval_jaxpr/ppermute | solution.py:14
  211.0 8.7 %collective-permute-start = (bf16[128,512]{1,0:T(8,128)(2,1)S(1)}, bf16[128,512]{1,0:T(8,128)(2,1)S(1)}, u32[]{:S(2)}, u32[]{:S(2)}) collective-permute-start(bf16[128,512]{1,0:T(8,128)(2,1)S(1)} %copy.21), channel_id=1, source_target_pairs={{0,1},{1,2},{2,3},{3,4},{4,5},{5,6},{6,7},{7,8},{8,9},{9,10},{10,1... | collective-permute-start | bytes 393224 | tf_op jit(solution)/shard_map/while/body/eval_jaxpr/ppermute | solution.py:14
  223.5 8.7 %collective-permute-start = (bf16[128,512]{1,0:T(8,128)(2,1)S(1)}, bf16[128,512]{1,0:T(8,128)(2,1)S(1)}, u32[]{:S(2)}, u32[]{:S(2)}) collective-permute-start(bf16[128,512]{1,0:T(8,128)(2,1)S(1)} %copy.21), channel_id=1, source_target_pairs={{0,1},{1,2},{2,3},{3,4},{4,5},{5,6},{6,7},{7,8},{8,9},{9,10},{10,1... | collective-permute-start | bytes 393224 | tf_op jit(solution)/shard_map/while/body/eval_jaxpr/ppermute | solution.py:14
  236.1 8.7 %collective-permute-start = (bf16[128,512]{1,0:T(8,128)(2,1)S(1)}, bf16[128,512]{1,0:T(8,128)(2,1)S(1)}, u32[]{:S(2)}, u32[]{:S(2)}) collective-permute-start(bf16[128,512]{1,0:T(8,128)(2,1)S(1)} %copy.21), channel_id=1, source_target_pairs={{0,1},{1,2},{2,3},{3,4},{4,5},{5,6},{6,7},{7,8},{8,9},{9,10},{10,1... | collective-permute-start | bytes 393224 | tf_op jit(solution)/shard_map/while/body/eval_jaxpr/ppermute | solution.py:14
  248.6 8.7 %collective-permute-start = (bf16[128,512]{1,0:T(8,128)(2,1)S(1)}, bf16[128,512]{1,0:T(8,128)(2,1)S(1)}, u32[]{:S(2)}, u32[]{:S(2)}) collective-permute-start(bf16[128,512]{1,0:T(8,128)(2,1)S(1)} %copy.21), channel_id=1, source_target_pairs={{0,1},{1,2},{2,3},{3,4},{4,5},{5,6},{6,7},{7,8},{8,9},{9,10},{10,1... | collective-permute-start | bytes 393224 | tf_op jit(solution)/shard_map/while/body/eval_jaxpr/ppermute | solution.py:14
  261.1 8.7 %collective-permute-start = (bf16[128,512]{1,0:T(8,128)(2,1)S(1)}, bf16[128,512]{1,0:T(8,128)(2,1)S(1)}, u32[]{:S(2)}, u32[]{:S(2)}) collective-permute-start(bf16[128,512]{1,0:T(8,128)(2,1)S(1)} %copy.21), channel_id=1, source_target_pairs={{0,1},{1,2},{2,3},{3,4},{4,5},{5,6},{6,7},{7,8},{8,9},{9,10},{10,1... | collective-permute-start | bytes 393224 | tf_op jit(solution)/shard_map/while/body/eval_jaxpr/ppermute | solution.py:14
  286.2 8.7 %collective-permute-start = (bf16[128,512]{1,0:T(8,128)(2,1)S(1)}, bf16[128,512]{1,0:T(8,128)(2,1)S(1)}, u32[]{:S(2)}, u32[]{:S(2)}) collective-permute-start(bf16[128,512]{1,0:T(8,128)(2,1)S(1)} %copy.21), channel_id=1, source_target_pairs={{0,1},{1,2},{2,3},{3,4},{4,5},{5,6},{6,7},{7,8},{8,9},{9,10},{10,1... | collective-permute-start | bytes 393224 | tf_op jit(solution)/shard_map/while/body/eval_jaxpr/ppermute | solution.py:14
  298.7 8.7 %collective-permute-start = (bf16[128,512]{1,0:T(8,128)(2,1)S(1)}, bf16[128,512]{1,0:T(8,128)(2,1)S(1)}, u32[]{:S(2)}, u32[]{:S(2)}) collective-permute-start(bf16[128,512]{1,0:T(8,128)(2,1)S(1)} %copy.21), channel_id=1, source_target_pairs={{0,1},{1,2},{2,3},{3,4},{4,5},{5,6},{6,7},{7,8},{8,9},{9,10},{10,1... | collective-permute-start | bytes 393224 | tf_op jit(solution)/shard_map/while/body/eval_jaxpr/ppermute | solution.py:14
  323.8 8.7 %collective-permute-start = (bf16[128,512]{1,0:T(8,128)(2,1)S(1)}, bf16[128,512]{1,0:T(8,128)(2,1)S(1)}, u32[]{:S(2)}, u32[]{:S(2)}) collective-permute-start(bf16[128,512]{1,0:T(8,128)(2,1)S(1)} %copy.21), channel_id=1, source_target_pairs={{0,1},{1,2},{2,3},{3,4},{4,5},{5,6},{6,7},{7,8},{8,9},{9,10},{10,1... | collective-permute-start | bytes 393224 | tf_op jit(solution)/shard_map/while/body/eval_jaxpr/ppermute | solution.py:14
  336.3 8.7 %collective-permute-start = (bf16[128,512]{1,0:T(8,128)(2,1)S(1)}, bf16[128,512]{1,0:T(8,128)(2,1)S(1)}, u32[]{:S(2)}, u32[]{:S(2)}) collective-permute-start(bf16[128,512]{1,0:T(8,128)(2,1)S(1)} %copy.21), channel_id=1, source_target_pairs={{0,1},{1,2},{2,3},{3,4},{4,5},{5,6},{6,7},{7,8},{8,9},{9,10},{10,1... | collective-permute-start | bytes 393224 | tf_op jit(solution)/shard_map/while/body/eval_jaxpr/ppermute | solution.py:14
  361.4 8.7 %collective-permute-start = (bf16[128,512]{1,0:T(8,128)(2,1)S(1)}, bf16[128,512]{1,0:T(8,128)(2,1)S(1)}, u32[]{:S(2)}, u32[]{:S(2)}) collective-permute-start(bf16[128,512]{1,0:T(8,128)(2,1)S(1)} %copy.21), channel_id=1, source_target_pairs={{0,1},{1,2},{2,3},{3,4},{4,5},{5,6},{6,7},{7,8},{8,9},{9,10},{10,1... | collective-permute-start | bytes 393224 | tf_op jit(solution)/shard_map/while/body/eval_jaxpr/ppermute | solution.py:14
  373.9 8.8 %collective-permute-start = (bf16[128,512]{1,0:T(8,128)(2,1)S(1)}, bf16[128,512]{1,0:T(8,128)(2,1)S(1)}, u32[]{:S(2)}, u32[]{:S(2)}) collective-permute-start(bf16[128,512]{1,0:T(8,128)(2,1)S(1)} %copy.21), channel_id=1, source_target_pairs={{0,1},{1,2},{2,3},{3,4},{4,5},{5,6},{6,7},{7,8},{8,9},{9,10},{10,1... | collective-permute-start | bytes 393224 | tf_op jit(solution)/shard_map/while/body/eval_jaxpr/ppermute | solution.py:14
  386.5 10.6 %collective-permute-start = (bf16[128,512]{1,0:T(8,128)(2,1)S(1)}, bf16[128,512]{1,0:T(8,128)(2,1)S(1)}, u32[]{:S(2)}, u32[]{:S(2)}) collective-permute-start(bf16[128,512]{1,0:T(8,128)(2,1)S(1)} %copy.21), channel_id=1, source_target_pairs={{0,1},{1,2},{2,3},{3,4},{4,5},{5,6},{6,7},{7,8},{8,9},{9,10},{10,1... | collective-permute-start | bytes 393224 | tf_op jit(solution)/shard_map/while/body/eval_jaxpr/ppermute | solution.py:14
  399.0 12.3 %collective-permute-start = (bf16[128,512]{1,0:T(8,128)(2,1)S(1)}, bf16[128,512]{1,0:T(8,128)(2,1)S(1)}, u32[]{:S(2)}, u32[]{:S(2)}) collective-permute-start(bf16[128,512]{1,0:T(8,128)(2,1)S(1)} %copy.21), channel_id=1, source_target_pairs={{0,1},{1,2},{2,3},{3,4},{4,5},{5,6},{6,7},{7,8},{8,9},{9,10},{10,1... | collective-permute-start | bytes 393224 | tf_op jit(solution)/shard_map/while/body/eval_jaxpr/ppermute | solution.py:14
  411.5 14.1 %collective-permute-start = (bf16[128,512]{1,0:T(8,128)(2,1)S(1)}, bf16[128,512]{1,0:T(8,128)(2,1)S(1)}, u32[]{:S(2)}, u32[]{:S(2)}) collective-permute-start(bf16[128,512]{1,0:T(8,128)(2,1)S(1)} %copy.21), channel_id=1, source_target_pairs={{0,1},{1,2},{2,3},{3,4},{4,5},{5,6},{6,7},{7,8},{8,9},{9,10},{10,1... | collective-permute-start | bytes 393224 | tf_op jit(solution)/shard_map/while/body/eval_jaxpr/ppermute | solution.py:14
  415.9 9.7 %collective-permute-start.1 = (f32[128,512]{1,0:T(8,128)}, f32[128,512]{1,0:T(8,128)S(1)}, u32[]{:S(2)}, u32[]{:S(2)}) collective-permute-start(f32[128,512]{1,0:T(8,128)} %fusion.42), channel_id=1, source_target_pairs={{0,1},{1,2},{2,3},{3,4},{4,5},{5,6},{6,7},{7,8},{8,9},{9,10},{10,1... | collective-permute-start | bytes 786440 | tf_op jit(solution)/shard_map/while/body/eval_jaxpr/ppermute | solution.py:14
  425.6 14.3 %collective-permute-start = (bf16[128,512]{1,0:T(8,128)(2,1)S(1)}, bf16[128,512]{1,0:T(8,128)(2,1)S(1)}, u32[]{:S(2)}, u32[]{:S(2)}) collective-permute-start(bf16[128,512]{1,0:T(8,128)(2,1)S(1)} %copy.21), channel_id=1, source_target_pairs={{0,1},{1,2},{2,3},{3,4},{4,5},{5,6},{6,7},{7,8},{8,9},{9,10},{10,1... | collective-permute-start | bytes 393224 | tf_op jit(solution)/shard_map/while/body/eval_jaxpr/ppermute | solution.py:14
  430.1 9.9 %collective-permute-start.1 = (f32[128,512]{1,0:T(8,128)}, f32[128,512]{1,0:T(8,128)S(1)}, u32[]{:S(2)}, u32[]{:S(2)}) collective-permute-start(f32[128,512]{1,0:T(8,128)} %fusion.42), channel_id=1, source_target_pairs={{0,1},{1,2},{2,3},{3,4},{4,5},{5,6},{6,7},{7,8},{8,9},{9,10},{10,1... | collective-permute-start | bytes 786440 | tf_op jit(solution)/shard_map/while/body/eval_jaxpr/ppermute | solution.py:14
  440.0 14.4 %collective-permute-start = (bf16[128,512]{1,0:T(8,128)(2,1)S(1)}, bf16[128,512]{1,0:T(8,128)(2,1)S(1)}, u32[]{:S(2)}, u32[]{:S(2)}) collective-permute-start(bf16[128,512]{1,0:T(8,128)(2,1)S(1)} %copy.21), channel_id=1, source_target_pairs={{0,1},{1,2},{2,3},{3,4},{4,5},{5,6},{6,7},{7,8},{8,9},{9,10},{10,1... | collective-permute-start | bytes 393224 | tf_op jit(solution)/shard_map/while/body/eval_jaxpr/ppermute | solution.py:14
  444.4 10.0 %collective-permute-start.1 = (f32[128,512]{1,0:T(8,128)}, f32[128,512]{1,0:T(8,128)S(1)}, u32[]{:S(2)}, u32[]{:S(2)}) collective-permute-start(f32[128,512]{1,0:T(8,128)} %fusion.42), channel_id=1, source_target_pairs={{0,1},{1,2},{2,3},{3,4},{4,5},{5,6},{6,7},{7,8},{8,9},{9,10},{10,1... | collective-permute-start | bytes 786440 | tf_op jit(solution)/shard_map/while/body/eval_jaxpr/ppermute | solution.py:14
  (38 other events, 509.9 us)
Sparse Core Ops, SparseCore 0:
  465.8 131.9 reduce-scatter.1
where the time goes:
time: 610 us; the launch traced here: 606 us
  waiting for transfers between devices  235 us (39%)
  other arithmetic  148 us (24%)
  matrix products  88 us (14%)
  local copies, waits for them, and re-layouts  45.8 us (8%)
  blocking collectives  45.3 us (7%)
  starting transfers between devices  27.2 us (4%)
  between operations  14.2 us (2%)
    reduce_scatter x1, waiting for transfers between devices, on_device(): lax.psum_scatter(grad_home, 'row', scatter_dimension=0, tiled=True)  128 us
    scatter-add x32, other arithmetic, padded_work(): region_totals = region_totals.at[rows_now].add(update)  124 us
    ppermute x63, waiting for transfers between devices, passed_along(): return lax.ppermute(value, axis, pairs)  107 us
    all_gather x1, blocking collectives, on_device(): panel_start = lax.all_gather(item_factors, 'row', axis=1, tiled=True)[0]  45.3 us
    dot_general x32, matrix products, padded_work(): jnp.einsum('sik,jk->sij', chosen, panel_now, preferred_element_type=jnp.f...  43.2 us
    dot_general x32, matrix products, padded_work(): jnp.einsum('sij,sik->jk', residual, chosen, preferred_element_type=jnp.fl...  32.7 us
    ppermute x63, starting transfers between devices, passed_along(): return lax.ppermute(value, axis, pairs)  27.1 us
    gather x32, local copies, waits for them, and re-layouts, padded_work(): chosen = jnp.take(region_blocks, rows_now, axis=0)  21.3 us
  transfers between devices with their start and end apart: 64, of which 30 were waited for; matrix products, arithmetic and copies ran while one was open for 45% of the time, Pallas kernels for 0%

commit v1 on v0

v1 whole, which is shorter than its diff:
```python
import functools

import jax
import jax.numpy as jnp
from jax import lax
from jax.experimental import pallas as pl
from jax.experimental.pallas import tpu as pltpu
from jax.sharding import PartitionSpec as P

region_rate = 0.05
item_rate = 0.01
decay_rate = 0.1

PANELS_PER_STEP = 4


def grad_kernel(rows_ref, counts_ref, u_ref, v_ref, slab_ref, region_ref, item_ref):
    step = pl.program_id(0)
    group = v_ref.shape[0]
    slots = slab_ref.shape[1]

    @pl.when(step == 0)
    def _():
        region_ref[...] = jnp.zeros_like(region_ref)

    for g in range(group):
        panel = step * group + g
        count = counts_ref[panel]
        v = v_ref[g]
        for s in range(slots):
            def slot_work(s=s, g=g, v=v, panel=panel):
                b = rows_ref[panel * slots + s]
                u = u_ref[b]
                predicted = lax.dot_general(
                    u, v, (((1,), (1,)), ((), ())), preferred_element_type=jnp.float32
                )
                residual = (predicted - slab_ref[g, s].astype(jnp.float32)).astype(jnp.bfloat16)
                region_ref[b] += jnp.dot(residual, v, preferred_element_type=jnp.float32)
                term = lax.dot_general(
                    residual, u, (((0,), (0,)), ((), ())), preferred_element_type=jnp.float32
                )
                if s == 0:
                    item_ref[g] = term
                else:
                    item_ref[g] += term

            if s == 0:
                slot_work()
            else:
                pl.when(s < count)(slot_work)

    @pl.when(step == pl.num_programs(0) - 1)
    def _():
        wide = u_ref[...].astype(jnp.float32)
        region_ref[...] = wide - region_rate * (region_ref[...] + decay_rate * wide)


def local_grads(region_blocks, panels, tiles, rows_flat, counts):
    row_blocks, block, width = region_blocks.shape
    n_panels, slots = tiles.shape[0], tiles.shape[1]
    group = PANELS_PER_STEP
    grid_spec = pltpu.PrefetchScalarGridSpec(
        num_scalar_prefetch=2,
        grid=(n_panels // group,),
        in_specs=[
            pl.BlockSpec((row_blocks, block, width), lambda i, r, c: (0, 0, 0)),
            pl.BlockSpec((group, block, width), lambda i, r, c: (i, 0, 0)),
            pl.BlockSpec((group, slots, block, block), lambda i, r, c: (i, 0, 0, 0)),
        ],
        out_specs=[
            pl.BlockSpec((row_blocks, block, width), lambda i, r, c: (0, 0, 0)),
            pl.BlockSpec((group, block, width), lambda i, r, c: (i, 0, 0)),
        ],
    )
    flops = 3 * 2 * n_panels * slots * block * block * width
    bytes_accessed = (
        region_blocks.size * 2 + panels.size * 2 + tiles.size * 2
        + region_blocks.size * 4 + panels.size * 4
    )
    return pl.pallas_call(
        grad_kernel,
        grid_spec=grid_spec,
        out_shape=[
            jax.ShapeDtypeStruct((row_blocks, block, width), jnp.float32),
            jax.ShapeDtypeStruct((n_panels, block, width), jnp.float32),
        ],
        compiler_params=pltpu.CompilerParams(
            dimension_semantics=("arbitrary",),
            vmem_limit_bytes=48 * 1024 * 1024,
        ),
        cost_estimate=pl.CostEstimate(
            flops=flops, bytes_accessed=bytes_accessed, transcendentals=0
        ),
    )(rows_flat, counts, region_blocks, panels, tiles)


def on_device(region_factors, item_factors, slab_blocks, block_rows, counts):
    block = slab_blocks.shape[-1]
    width = region_factors.shape[-1]
    row_blocks = region_factors.shape[0] // block
    n_panels = slab_blocks.shape[1]
    region_blocks = region_factors.reshape(row_blocks, block, width)
    panel_own = lax.all_gather(item_factors, "row", axis=1, tiled=True)
    panels = lax.all_gather(panel_own, "col", axis=0, tiled=True)
    new_regions, item_part = local_grads(
        region_blocks, panels, slab_blocks[0], block_rows[0].reshape(-1), counts[0]
    )
    pieces = lax.axis_size("row")
    piece = block // pieces
    item_part = item_part.reshape(n_panels * pieces, piece, width)
    own_grad = lax.psum_scatter(item_part, ("col", "row"), scatter_dimension=0, tiled=True)
    own_rows = item_factors.astype(jnp.float32)
    new_items = own_rows - item_rate * (own_grad + decay_rate * own_rows)
    return (new_regions.reshape(row_blocks * block, width), new_items)


def solution(mesh):
    return jax.shard_map(
        on_device,
        mesh=mesh,
        in_specs=(
            P(("row", "col"), None),
            P("col", "row", None),
            P(("row", "col"), None, None, None, None),
            P(("row", "col"), None, None),
            P(("row", "col"), None),
        ),
        out_specs=(P(("row", "col"), None), P("col", "row", None)),
        check_vma=False,
    )
```

time: 610 us -> 1700 us (2.79)
  waiting for transfers between devices: 235 us -> 1580 us
  other arithmetic: 148 us -> 1.38 us
  matrix products: 88 us -> 0 us
  Pallas kernels: 0 us -> 56.6 us
  local copies, waits for them, and re-layouts: 45.8 us -> 4.94 us
  starting transfers between devices: 27.2 us -> 0.08 us
    reduce_scatter x1, waiting for transfers between devices: 128 us -> 1510 us  [on_device(): lax.psum_scatter(item_part, ('col', 'row'), scatter_dimension=0, tiled=True)]
    scatter-add x32 -> x0, other arithmetic: 124 us -> none  [padded_work(): region_totals = region_totals.at[rows_now].add(update)]
    ppermute x63 -> x0, waiting for transfers between devices: 107 us -> none  [passed_along(): return lax.ppermute(value, axis, pairs)]
    dot_general x96 -> x0, matrix products: 88 us -> none  [the longest x32 43.2 us: padded_work(): jnp.einsum('sik,jk->sij', chosen, panel_now, preferred_element_type=jnp.f...]
    all_gather x0 -> x1, waiting for transfers between devices: none -> 62.9 us  [on_device(): panels = lax.all_gather(panel_own, 'col', axis=0, tiled=True)]
    pallas_call x0 -> x1, Pallas kernels: none -> 56.6 us  [local_grads(): pl.pallas_call(grad_kernel, grid_spec=grid_spec, out_shape=[jax.ShapeDtyp...]
    ppermute x63 -> x0, starting transfers between devices: 27.1 us -> none  [passed_along(): return lax.ppermute(value, axis, pairs)]
    gather x32 -> x0, local copies, waits for them, and re-layouts: 21.3 us -> none  [padded_work(): chosen = jnp.take(region_blocks, rows_now, axis=0)]
  transfers between devices with their start and end apart: 64 -> 2, of which waited for: 30 -> 2; matrix products, arithmetic and copies ran while one was open for 45% -> 0% of each run, Pallas kernels for 0% -> 0%
where the time goes in v1:
time: 1700 us
  waiting for transfers between devices  1580 us (93%)
  Pallas kernels  56.6 us (3%)
  blocking collectives  47.3 us (3%)
    reduce_scatter x1, waiting for transfers between devices, on_device(): lax.psum_scatter(item_part, ('col', 'row'), scatter_dimension=0, tiled=True)  1510 us
    all_gather x1, waiting for transfers between devices, on_device(): panels = lax.all_gather(panel_own, 'col', axis=0, tiled=True)  62.9 us
    pallas_call x1, Pallas kernels, local_grads(): pl.pallas_call(grad_kernel, grid_spec=grid_spec, out_shape=[jax.ShapeDtyp...  56.6 us
    all_gather x1, blocking collectives, on_device(): panel_own = lax.all_gather(item_factors, 'row', axis=1, tiled=True)  47.3 us
  transfers between devices with their start and end apart: 2, of which 2 were waited for; matrix products, arithmetic and copies ran while one was open for 0% of the time, Pallas kernels for 0%

profile of v1, /device:TPU:32, one launch (start us, length us, event | category | flops | bytes accessed | tf_op | source)
XLA Modules:
  0.0 1699.9 jit_solution(4250228837046134425)
XLA Ops:
  7.2 0.0 all-gather.2.cloned.1.call-start
  7.2 47.3 %all_gather.6 = bf16[1,128,512]{2,1,0:T(8,128)(2,1)} all-gather(bf16[1,16,512]{2,1,0:T(8,128)(2,1)} %param.6), channel_id=1, replica_groups=mesh['row'=8,'col'=32] {'row'}, dimensions={1}, use_global_device_ids=true | all-gather | bytes 147456 | tf_op jit(solution)/shard_map/all_gather | solution.py:103
  54.5 0.0 all-gather.2.cloned.1.call-update
  54.5 0.0 reduce-scatter.2.cloned.1.call-start
  54.6 0.8 copy.8
  55.3 0.1 reshape_squeeze.3.rows_ref
  55.4 62.9 %all-gather.2.cloned.1.call-done.v_ref = bf16[32,128,512]{2,1,0:T(8,128)(2,1)} async-done(((bf16[1,128,512]{2,1,0:T(8,128)(2,1)}), bf16[32,128,512]{2,1,0:T(8,128)(2,1)}) %all-gather.2.cloned.1.call-update) | async-done | bytes 4194320 | tf_op jit(solution)/shard_map/all_gather | solution.py:104
  118.3 0.0 copy-start
  118.3 2.2 copy-done
  120.5 0.0 copy-start.1
  120.5 1.2 copy-done.1
  121.7 0.0 copy-start.2
  121.7 0.7 copy-done.2
  122.4 56.6 %shard_map.68 = (f32[8,128,512]{2,1,0:T(8,128)}, f32[32,128,512]{2,1,0:T(8,128)}) custom-call(s32[192]{0:T(256)S(1)} %reshape_squeeze.3.rows_ref, s32[32]{0:T(128)S(1)} %bitcast.6, bf16[8,128,512]{2,1,0:T(8,128)(2,1)S(1)} %bitcast.5, bf16[32,128,512]{2,1,0:T(8,128)(2,1)S(1)} %copy-done, bf16[32,6,128,128]{3,2,1,0:T(8,128)(2,1)} %bitcast.8), custom_call_target="tpu_custom_call" | custom-call | flops 9663676416 | bytes 22020096 | tf_op jit(solution)/shard_map/pallas_call | solution.py:80
  179.0 0.0 copy-start.3
  179.0 0.0 reduce-scatter.2.cloned.1.call-update
  179.0 1512.7 %reduce-scatter.2.cloned.1.call-done = f32[1,16,512]{2,1,0:T(8,128)} async-done(((f32[256,16,512]{2,1,0:T(8,128)}), f32[1,16,512]{2,1,0:T(8,128)}) %reduce-scatter.2.cloned.1.call-update) | async-done | bytes 32784 | tf_op jit(solution)/shard_map/reduce_scatter | solution.py:111
  1691.7 0.0 copy-done.3
  1691.7 1.4 convert_subtract_fusion
Async XLA Ops:
  7.2 111.2 %all-gather.2.cloned.1.call-start = ((), (), s32[]{:S(2)}) async-start(), calls=%async_computation.1 | async-start | bytes 4325376 | tf_op jit(solution)/shard_map/all_gather | solution.py:104
  54.5 1637.1 %reduce-scatter.2.cloned.1.call-start = ((), (), s32[]{:S(2)}) async-start(), calls=%async_computation.2 | async-start | bytes 8421376 | tf_op jit(solution)/shard_map/reduce_scatter | solution.py:111
  118.3 2.2 copy-start
  120.5 1.2 copy-start.1
  121.7 0.7 copy-start.2
  179.0 1512.7 %copy-start.3 = (bf16[1,16,512]{2,1,0:T(8,128)(2,1)S(1)}, bf16[1,16,512]{2,1,0:T(8,128)(2,1)}, u32[]{:S(2)}) copy-start(bf16[1,16,512]{2,1,0:T(8,128)(2,1)} %param.6) | copy-start | bytes 49156
Sparse Core Ops, SparseCore 0:
  54.6 63.6 all-gather.1
  179.1 1512.5 reduce-scatter.1
